TPU v7x, 512 devices: a whole 4x8x8 slice. The times are simulated.
512 devices in a mesh: dp: 16 (over y, core), cell: 32 (over x, z).
Axes of the slice: x: 4, y: 8, z: 8, core: 2. Of those that a mesh axis runs over, the one named last changes fastest.
Arguments:
- sensitivity: bfloat16 [2048, 200704], P('dp', 'cell'), may hold values from -0.0390625 to 0.0390625
- direction: bfloat16 [16, 200704], P(None, 'cell'), may hold values from -6 to 6
- depth_weight: float32 [200704], P('cell'), may hold values from 0.3 to 3
- counts: int32 [32], P('cell'), may hold values from 4704 to 6272, as said below
- send_lists: int32 [32, 2, 128], P('cell'), may hold values from 0 to 6271, as said below
- neighbours: int32 [6, 200704], P(None, 'cell'), may hold values from 0 to 6528, as said below
Outputs:
- product: float32 [16, 200704], P(None, 'cell')
Inputs may be any that keep to these rules, and one draw needn't show every extreme that they name: `counts`: every partition has at least 4704 live cells; some partition is full in every draw. `send_lists`: entries are local indices of live cells of their own partition. `neighbours`: entries below 6272 are live local cells that differ from the cell's own local index by at most 64; 6272 to 6527 name received rim cells; 6528 is an absent face; padded slots hold only absent faces.
All inputs are finite; a program needn't handle non-finite values.
Results may differ from a plain program's by a relative error of at most 0.0008.
Values sent between devices are 32-bit elements; how exact they have to be, the bound alone decides.
No kernel may reach another device: no remote copies, remote signals or barrier semaphores. Data moves between devices by JAX's collectives and lax.ppermute only.
A program may use at most 64 MiB of HBM per device.

v0:
```python
import jax
import jax.numpy as jnp
from jax import lax
from jax.sharding import PartitionSpec as P


def padded_2(value, sides, width):
    for axis, dim in sides:
        count, length = (lax.axis_size(axis), value.shape[dim])
        up = [(i, (i + 1) % count) for i in range(count - 1)]
        down = [(j, i) for i, j in up]
        last = lax.slice_in_dim(value, length - width, length, axis=dim)
        leading = lax.slice_in_dim(value, 0, width, axis=dim)
        before = lax.ppermute(last, axis, up)
        after = lax.ppermute(leading, axis, down)
        value = jnp.concatenate([before, value, after], axis=dim)
    return value


def pick_block():
    block_len = 8
    for candidate in range(128, 7, -8):
        block_len = candidate
        break
    return block_len


def pick_group(block_count):
    group_len = 1
    for candidate in range(1, 9):
        if block_count % candidate == 0:
            group_len = candidate
    return group_len


def smoothness(masked_f, weight, send_lists, neighbours, width):
    slots = masked_f.shape[1]
    values = jnp.concatenate([masked_f * weight[None, :], weight[None, :]], axis=0)
    picked = jnp.take(values, send_lists[0].reshape(-1), axis=1)
    rim = picked.shape[1] // 2
    padded = padded_2(picked, (("cell", 1),), rim)
    rim_vals = jnp.concatenate([padded[:, :rim], padded[:, 3 * rim :]], axis=1)
    lanes = values.shape[0]
    block_len = pick_block()
    block_count = width // block_len
    pieces = 1 + (128 + block_len - 1) // block_len
    spread = jnp.pad(values, ((0, 0), (64, pieces * block_len)))
    local_vals = lax.slice_in_dim(spread, 0, (block_count + pieces - 1) * block_len, axis=1)
    shifted = [
        local_vals[:, m * block_len : (m + block_count) * block_len].reshape(
            lanes, block_count, block_len
        )
        for m in range(pieces)
    ]
    rim_part = jnp.broadcast_to(rim_vals[:, None, :], (lanes, block_count, 2 * rim))
    windows = jnp.concatenate(shifted + [rim_part], axis=2).transpose(1, 0, 2)
    span = windows.shape[2]
    position = jnp.arange(width, dtype=jnp.int32)
    anchor = position // block_len * block_len
    column = jnp.where(
        neighbours < slots,
        neighbours - anchor[None, :] + 64,
        jnp.where(neighbours < slots + 2 * rim, pieces * block_len + neighbours - slots, -1),
    )
    column = column.reshape(neighbours.shape[0], block_count, block_len).transpose(1, 0, 2)
    group_len = pick_group(block_count)
    windows = windows.reshape(block_count // group_len, group_len, lanes, span)
    column = column.reshape(block_count // group_len, group_len, neighbours.shape[0], block_len)

    def gather_block(item):
        window_set, column_set = item
        target = jnp.arange(span, dtype=jnp.int32)[None, None, :, None]
        hits = jnp.sum((column_set[:, :, None, :] == target).astype(jnp.float32), axis=1)
        return jnp.einsum("grw,gwb->grb", window_set, hits, precision=lax.Precision.HIGHEST)

    sums = lax.map(gather_block, (windows, column))
    sums = sums.reshape(block_count, lanes, block_len).transpose(1, 0, 2).reshape(lanes, width)
    coupling = masked_f * sums[-1][None, :] - sums[:-1]
    return weight[None] * weight[None] * masked_f + weight[None] * coupling


def on_device(sensitivity, direction, depth_weight, counts, send_lists, neighbours):
    slots = sensitivity.shape[1]
    nvecs = direction.shape[0]
    live = jnp.arange(slots, dtype=jnp.int32) < counts[0]
    masked = jnp.where(live[None, :], direction, jnp.zeros_like(direction))
    partial_data = lax.dot_general(
        masked, sensitivity, (((1,), (1,)), ((), ())), preferred_element_type=jnp.float32
    )
    summed = lax.psum(partial_data, "cell")
    rounded = summed.astype(jnp.bfloat16)
    remainder = (summed - rounded.astype(jnp.float32)).astype(jnp.bfloat16)
    stacked = jnp.concatenate([rounded, remainder], axis=0)
    both = jnp.dot(stacked, sensitivity, preferred_element_type=jnp.float32)
    partial_cells = both[:nvecs] + both[nvecs:]
    weight = jnp.where(live, depth_weight, jnp.float32(0.0))
    masked_f = masked.astype(jnp.float32)
    misfit = lax.psum(partial_cells, "dp")
    smooth = smoothness(masked_f, weight, send_lists, neighbours, slots)
    total = misfit + 0.5 * smooth
    return jnp.where(live[None, :], total, jnp.float32(0.0))


def solution(mesh):
    placed = (
        P("dp", "cell"),
        P(None, "cell"),
        P("cell"),
        P("cell"),
        P("cell", None, None),
        P(None, "cell"),
    )
    return jax.shard_map(
        on_device, mesh=mesh, in_specs=placed, out_specs=P(None, "cell"), check_vma=False
    )
```

profile of v0, /device:TPU:1, one launch (start us, length us, event | category | flops | bytes accessed | tf_op | source)
XLA Modules:
  0.0 220.8 jit_solution(9854497497350042663)
XLA Ops:
  6.5 0.0 copy-start
  6.5 0.0 all-reduce.3.cloned.1.call-start
  7.3 0.8 fusion.22
  8.1 1.0 convert_multiply_fusion.1
  9.1 0.0 copy-start.5
  9.1 0.1 pad_maximum_fusion.1
  9.2 0.0 copy-start.1
  9.2 2.3 %copy.26 = f32[17,6272]{0,1:T(8,128)} copy(f32[17,6272]{1,0:T(8,128)S(1)} %pad_maximum_fusion.1) | data formatting | bytes 852992 | tf_op jit(solution)/shard_map/concatenate | solution.py:38
  11.5 0.0 copy-done.5
  11.6 2.6 %gather_fusion = f32[256,17]{1,0:T(8,128)S(1)} fusion(f32[17,6272]{0,1:T(8,128)} %copy.26, s32[1024]{0:T(1024)S(1)} %pad_clamp_fusion), kind=kCustom, calls=%fused_computation | custom fusion | bytes 35840 | tf_op jit(solution)/shard_map/jit(_take)/gather | solution.py:39
  14.2 0.1 select_bitcast_fusion
  14.3 0.7 fusion.23
  14.9 5.4 %collective-permute-start = (f32[17,128]{0,1:T(8,128)}, f32[17,128]{0,1:T(8,128)}, u32[]{:S(2)}, u32[]{:S(2)}) collective-permute-start(f32[17,128]{0,1:T(8,128)} %get-tuple-element.42), channel_id=1, source_target_pairs={{0,1},{1,2},{2,3},{3,4},{4,5},{5,6},{6,7},{7,8},{8,9},{9,10},{10,1... | collective-permute-start | bytes 26120 | tf_op jit(solution)/shard_map/ppermute | solution.py:14
  20.4 1.3 collective-permute-start.1
  21.6 0.0 copy-done
  21.7 0.0 copy-done.1
  21.7 0.5 fusion.10
  22.2 0.0 copy-start.4
  22.2 67.6 %psum.14 = f32[16,128]{1,0:T(8,128)S(1)} all-reduce(f32[16,128]{1,0:T(8,128)S(1)} %fusion.10), channel_id=1, replica_groups=mesh['dp'=16,'cell'=32] {'cell'}, use_global_device_ids=true, to_apply=%region_0.1 | all-reduce | flops 2048 | bytes 16384 | tf_op jit(solution)/shard_map/psum | solution.py:90
  89.8 0.4 fusion.16
  90.1 0.8 slice_add_fusion
  90.9 0.0 all-reduce.3.cloned.1.call-update
  91.0 0.0 copy-done.4
  91.0 0.7 select_select_fusion
  91.7 0.4 pad_slice_fusion.1
  92.1 0.8 reshape.80
  92.9 1.1 copy.29
  94.1 0.1 reshape.81
  94.1 0.1 copy.30
  94.2 0.0 collective-permute-done
  94.2 0.9 copy.27
  95.2 0.0 collective-permute-done.1
  95.2 0.1 copy.28
  95.3 0.1 broadcast_in_dim.71
  95.4 0.0 copy-start.3
  95.4 1.7 pad_maximum_fusion
  97.1 0.0 copy-done.3
  97.1 0.0 copy-start.2
  97.1 30.0 %while.10 = (s32[]{:T(128)}, f32[7,7,17,128]{3,2,1,0:T(8,128)S(1)}, f32[7,7,17,512]{3,2,1,0:T(8,128)}, s32[7,7,6,128]{3,2,1,0:T(8,128)}, s32[]{:T(128)}) while((s32[]{:T(128)}, f32[7,7,17,128]{3,2,1,0:T(8,128)S(1)}, f32[7,7,17,512]{3,2,1,0:T(8,128)}, s32[7,7,6,128]{3,2,1,0:T(8,128)}, s32[]{:T(128)}) %tuple.29), condition=%wide.region_4.5_spmd, body=%wide.region_2.4_spmd.sunk | while | flops 101384192 | bytes 4165697 | solution.py:76
  97.1 0.8 dynamic-slice_bitcast_fusion.2
  97.9 1.5 convert_reduce_fusion.2
  99.4 2.0 fusion.32
  101.4 0.8 dynamic-slice_bitcast_fusion.2
  102.2 1.5 convert_reduce_fusion.2
  103.7 2.0 fusion.32
  105.7 0.8 dynamic-slice_bitcast_fusion.2
  106.5 1.5 convert_reduce_fusion.2
  107.9 2.0 fusion.32
  110.0 0.8 dynamic-slice_bitcast_fusion.2
  110.8 1.5 convert_reduce_fusion.2
  112.2 2.0 fusion.32
  114.3 0.8 dynamic-slice_bitcast_fusion.2
  115.0 1.5 convert_reduce_fusion.2
  116.5 2.0 fusion.32
  118.6 0.8 dynamic-slice_bitcast_fusion.2
  119.3 1.5 convert_reduce_fusion.2
  120.8 2.0 fusion.32
  122.8 0.8 dynamic-slice_bitcast_fusion.2
  123.6 1.5 convert_reduce_fusion.2
  125.1 2.0 fusion.32
  127.1 0.1 copy.36
  127.3 84.8 %all-reduce.3.cloned.1.call-done = f32[16,6272]{1,0:T(8,128)} async-done(((f32[16,6272]{1,0:T(8,128)}), f32[16,6272]{1,0:T(8,128)}) %all-reduce.3.cloned.1.call-update) | async-done | bytes 401424 | tf_op jit(solution)/shard_map/psum | solution.py:98
  212.1 0.0 copy-done.2
  212.1 1.9 fusion.7
  (11 shorter events, 0.1 us)
Async XLA Ops:
  6.5 15.1 %copy-start = (bf16[128,6272]{1,0:T(8,128)(2,1)S(1)}, bf16[128,6272]{1,0:T(8,128)(2,1)}, u32[]{:S(2)}) copy-start(bf16[128,6272]{1,0:T(8,128)(2,1)} %param.8) | copy-start | bytes 4816900
  6.5 205.5 %all-reduce.3.cloned.1.call-start = ((), (), s32[]{:S(2)}) async-start(), calls=%async_computation | async-start | bytes 802816 | tf_op jit(solution)/shard_map/psum | solution.py:98
  9.1 2.4 %copy-start.5 = (s32[1,2,128]{2,1,0:T(2,128)S(1)}, s32[1,2,128]{2,1,0:T(2,128)}, u32[]{:S(2)}) copy-start(s32[1,2,128]{2,1,0:T(2,128)} %param.12) | copy-start | bytes 3076
  9.2 12.5 %copy-start.1 = (bf16[16,6272]{1,0:T(8,128)(2,1)S(1)}, bf16[16,6272]{1,0:T(8,128)(2,1)}, u32[]{:S(2)}) copy-start(bf16[16,6272]{1,0:T(8,128)(2,1)} %param.9) | copy-start | bytes 602116
  14.9 79.3 %collective-permute-start = (f32[17,128]{0,1:T(8,128)}, f32[17,128]{0,1:T(8,128)}, u32[]{:S(2)}, u32[]{:S(2)}) collective-permute-start(f32[17,128]{0,1:T(8,128)} %get-tuple-element.42), channel_id=1, source_target_pairs={{0,1},{1,2},{2,3},{3,4},{4,5},{5,6},{6,7},{7,8},{8,9},{9,10},{10,1... | collective-permute-start | bytes 26120 | tf_op jit(solution)/shard_map/ppermute | solution.py:14
  20.4 74.8 %collective-permute-start.1 = (f32[17,128]{0,1:T(8,128)}, f32[17,128]{0,1:T(8,128)S(1)}, u32[]{:S(2)}, u32[]{:S(2)}) collective-permute-start(f32[17,128]{0,1:T(8,128)} %get-tuple-element.43), channel_id=1, source_target_pairs={{1,0},{2,1},{3,2},{4,3},{5,4},{6,5},{7,6},{8,7},{9,8},{10,9},{11,1... | collective-permute-start | bytes 26120 | tf_op jit(solution)/shard_map/ppermute | solution.py:15
  22.2 68.8 %copy-start.4 = (s32[6,6272]{1,0:T(8,128)S(1)}, s32[6,6272]{1,0:T(8,128)}, u32[]{:S(2)}) copy-start(s32[6,6272]{1,0:T(8,128)} %param.13) | copy-start | bytes 451588
  95.4 1.8 copy-start.3
  97.1 115.0 %copy-start.2 = (bf16[16,6272]{1,0:T(8,128)(2,1)S(1)}, bf16[16,6272]{1,0:T(8,128)(2,1)}, u32[]{:S(2)}) copy-start(bf16[16,6272]{1,0:T(8,128)(2,1)} %param.9) | copy-start | bytes 602116
Sparse Core Ops, SparseCore 0:
  91.1 120.9 all-reduce.2
where the time goes:
time: 222 us; the launch traced here: 221 us
  waiting for transfers between devices  84.8 us (38%)
  blocking collectives  67.6 us (30%)
  other arithmetic  17.4 us (8%)
  matrix products  15 us (7%)
  local copies, waits for them, and re-layouts  14.7 us (7%)
  between operations  14.4 us (6%)
  starting transfers between devices  6.7 us (3%)
    psum x1, waiting for transfers between devices, on_device(): misfit = lax.psum(partial_cells, 'dp')  84.8 us
    psum x1, blocking collectives, on_device(): summed = lax.psum(partial_data, 'cell')  67.6 us
    dot_general x7, matrix products, gather_block(): jnp.einsum('grw,gwb->grb', window_set, hits, precision=lax.Precision.HIGH...  14.2 us
    reduce_sum x7, other arithmetic, gather_block(): jnp.sum((column_set[:, :, None, :] == target).astype(jnp.float32), axis=1)  10.3 us
    ppermute x1, starting transfers between devices, padded_2(): before = lax.ppermute(last, axis, up)  5.42 us
    eq x7, local copies, waits for them, and re-layouts, gather_block(): column_set[:, :, None, :] == target  5.32 us
  transfers between devices with their start and end apart: 3, of which 1 were waited for; matrix products, arithmetic and copies ran while one was open for 17% of the time, Pallas kernels for 0%

commit v1 on v0

--- a/solution.py
+++ b/solution.py
@@ -2,6 +2,14 @@
 import jax.numpy as jnp
 from jax import lax
 from jax.sharding import PartitionSpec as P
+
+
+def add_in_pairs(value, name):
+    count, total = (lax.axis_size(name), value)
+    for reach in [1 << k for k in range(count.bit_length() - 1)]:
+        pairs = [(i, i ^ reach) for i in range(count)]
+        total = total + lax.ppermute(total, name, pairs)
+    return total
 
 
 def padded_2(value, sides, width):
@@ -87,7 +95,7 @@
     partial_data = lax.dot_general(
         masked, sensitivity, (((1,), (1,)), ((), ())), preferred_element_type=jnp.float32
     )
-    summed = lax.psum(partial_data, "cell")
+    summed = add_in_pairs(partial_data, "cell")
     rounded = summed.astype(jnp.bfloat16)
     remainder = (summed - rounded.astype(jnp.float32)).astype(jnp.bfloat16)
     stacked = jnp.concatenate([rounded, remainder], axis=0)

time: 222 us -> 213 us (0.959)
  blocking collectives: 67.6 us -> 0 us
  waiting for transfers between devices: 84.8 us -> 116 us
  starting transfers between devices: 6.7 us -> 32.5 us
    psum x1 -> x0, blocking collectives: 67.6 us -> none  [on_device(): summed = lax.psum(partial_data, 'cell')]
    psum x1, waiting for transfers between devices: 84.8 us -> 114 us  [on_device(): misfit = lax.psum(partial_cells, 'dp')]
    ppermute x0 -> x5, starting transfers between devices: none -> 28.7 us  [add_in_pairs(): total = total + lax.ppermute(total, name, pairs)]
    ppermute x1, starting transfers between devices: 5.42 us -> 2.54 us  [padded_2(): before = lax.ppermute(last, axis, up)]
  transfers between devices with their start and end apart: 3 -> 8, of which waited for: 1 -> 2; matrix products, arithmetic and copies ran while one was open for 17% -> 21% of each run, Pallas kernels for 0% -> 0%
where the time goes in v1:
time: 213 us; the launch traced here: 212 us
  waiting for transfers between devices  116 us (54%)
  starting transfers between devices  32.5 us (15%)
  other arithmetic  18.2 us (9%)
  matrix products  15.9 us (7%)
  local copies, waits for them, and re-layouts  15.3 us (7%)
  between operations  14.4 us (7%)
    psum x1, waiting for transfers between devices, on_device(): misfit = lax.psum(partial_cells, 'dp')  114 us
    ppermute x5, starting transfers between devices, add_in_pairs(): total = total + lax.ppermute(total, name, pairs)  28.7 us
    dot_general x7, matrix products, gather_block(): jnp.einsum('grw,gwb->grb', window_set, hits, precision=lax.Precision.HIGH...  14.2 us
    reduce_sum x7, other arithmetic, gather_block(): jnp.sum((column_set[:, :, None, :] == target).astype(jnp.float32), axis=1)  10.3 us
    eq x7, local copies, waits for them, and re-layouts, gather_block(): column_set[:, :, None, :] == target  5.28 us
  transfers between devices with their start and end apart: 8, of which 2 were waited for; matrix products, arithmetic and copies ran while one was open for 21% of the time, Pallas kernels for 0%

profile of v1, /device:TPU:1, one launch (start us, length us, event | category | flops | bytes accessed | tf_op | source)
XLA Modules:
  0.0 212.1 jit_solution(7319139454436700179)
XLA Ops:
  7.3 0.6 copy-done
  8.0 1.4 fusion.10
  9.4 4.9 %collective-permute-start = (f32[16,128]{1,0:T(8,128)S(1)}, f32[16,128]{1,0:T(8,128)S(1)}, u32[]{:S(2)}, u32[]{:S(2)}) collective-permute-start(f32[16,128]{1,0:T(8,128)S(1)} %fusion.10), channel_id=1, source_target_pairs={{0,1},{1,0},{2,3},{3,2},{4,5},{5,4},{6,7},{7,6},{8,9},{9,8},{10,11... | collective-permute-start | bytes 24584 | tf_op jit(solution)/shard_map/ppermute | solution.py:11
  14.3 0.8 fusion.22
  15.0 1.0 convert_multiply_fusion.1
  16.0 0.0 copy-start.4
  16.1 0.1 pad_maximum_fusion.1
  16.1 0.0 copy-start.3
  16.1 2.3 %copy.26 = f32[17,6272]{0,1:T(8,128)} copy(f32[17,6272]{1,0:T(8,128)S(1)} %pad_maximum_fusion.1) | data formatting | bytes 852992 | tf_op jit(solution)/shard_map/concatenate | solution.py:46
  18.5 2.6 %gather_fusion = f32[256,17]{1,0:T(8,128)S(1)} fusion(f32[17,6272]{0,1:T(8,128)} %copy.26, s32[1024]{0:T(1024)S(1)} %pad_clamp_fusion), kind=kCustom, calls=%fused_computation | custom fusion | bytes 35840 | tf_op jit(solution)/shard_map/jit(_take)/gather | solution.py:47
  21.1 0.1 select_bitcast_fusion
  21.2 0.7 fusion.23
  21.9 2.5 %collective-permute-start.5 = (f32[17,128]{0,1:T(8,128)}, f32[17,128]{0,1:T(8,128)}, u32[]{:S(2)}, u32[]{:S(2)}) collective-permute-start(f32[17,128]{0,1:T(8,128)} %get-tuple-element.40), channel_id=1, source_target_pairs={{0,1},{1,2},{2,3},{3,4},{4,5},{5,6},{6,7},{7,8},{8,9},{9,10},{10,1... | collective-permute-start | bytes 26120 | tf_op jit(solution)/shard_map/ppermute | solution.py:22
  24.4 1.3 collective-permute-start.6
  25.7 0.7 select_select_fusion
  26.5 0.0 collective-permute-done
  26.5 7.3 %collective-permute-start.1 = (f32[16,128]{1,0:T(8,128)S(1)}, f32[16,128]{1,0:T(8,128)}, u32[]{:S(2)}, u32[]{:S(2)}) collective-permute-start(f32[16,128]{1,0:T(8,128)S(1)} %add.68), channel_id=1, source_target_pairs={{0,2},{1,3},{2,0},{3,1},{4,6},{5,7},{6,4},{7,5},{8,10},{9,11},{10,... | collective-permute-start | bytes 24584 | tf_op jit(solution)/shard_map/ppermute | solution.py:11
  33.7 0.4 pad_slice_fusion.1
  34.1 0.9 reshape.80
  35.0 1.1 copy.29
  36.1 0.1 reshape.81
  36.2 0.1 copy.30
  36.3 0.0 collective-permute-done.5
  36.3 0.9 copy.27
  37.2 0.0 collective-permute-done.6
  37.2 0.1 copy.28
  37.3 0.0 collective-permute-done.1
  37.3 0.7 add.69
  38.0 7.9 %collective-permute-start.2 = (f32[16,128]{1,0:T(8,128)S(1)}, f32[16,128]{1,0:T(8,128)S(1)}, u32[]{:S(2)}, u32[]{:S(2)}) collective-permute-start(f32[16,128]{1,0:T(8,128)S(1)} %add.69), channel_id=1, source_target_pairs={{0,4},{1,5},{2,6},{3,7},{4,0},{5,1},{6,2},{7,3},{8,12},{9,13},{10,... | collective-permute-start | bytes 24584 | tf_op jit(solution)/shard_map/ppermute | solution.py:11
  46.0 1.0 collective-permute-done.2
  47.0 4.0 %collective-permute-start.3 = (f32[16,128]{1,0:T(8,128)S(1)}, f32[16,128]{1,0:T(8,128)S(1)}, u32[]{:S(2)}, u32[]{:S(2)}) collective-permute-start(f32[16,128]{1,0:T(8,128)S(1)} %add.70), channel_id=1, source_target_pairs={{0,8},{1,9},{2,10},{3,11},{4,12},{5,13},{6,14},{7,15},{8,0},{9,1},... | collective-permute-start | bytes 24584 | tf_op jit(solution)/shard_map/ppermute | solution.py:11
  51.0 0.1 broadcast_in_dim.71
  51.1 1.8 pad_maximum_fusion
  52.9 0.0 collective-permute-done.3
  52.9 4.6 %collective-permute-start.4 = (f32[16,128]{1,0:T(8,128)S(1)}, f32[16,128]{1,0:T(8,128)S(1)}, u32[]{:S(2)}, u32[]{:S(2)}) collective-permute-start(f32[16,128]{1,0:T(8,128)S(1)} %add.71), channel_id=1, source_target_pairs={{0,16},{1,17},{2,18},{3,19},{4,20},{5,21},{6,22},{7,23},{8,24},{9,... | collective-permute-start | bytes 24584 | tf_op jit(solution)/shard_map/ppermute | solution.py:11
  57.5 30.0 %while.10 = (s32[]{:T(128)}, f32[7,7,17,128]{3,2,1,0:T(8,128)S(1)}, f32[7,7,17,512]{3,2,1,0:T(8,128)}, s32[7,7,6,128]{3,2,1,0:T(8,128)}, s32[]{:T(128)}) while((s32[]{:T(128)}, f32[7,7,17,128]{3,2,1,0:T(8,128)S(1)}, f32[7,7,17,512]{3,2,1,0:T(8,128)}, s32[7,7,6,128]{3,2,1,0:T(8,128)}, s32[]{:T(128)}) %tuple.29), condition=%wide.region_3.4_spmd, body=%wide.region_1.3_spmd.sunk | while | flops 101384192 | bytes 4165697 | solution.py:84
  57.5 0.8 dynamic-slice_bitcast_fusion.2
  58.3 1.5 convert_reduce_fusion.2
  59.8 2.0 fusion.32
  61.8 0.8 dynamic-slice_bitcast_fusion.2
  62.6 1.5 convert_reduce_fusion.2
  64.1 2.0 fusion.32
  66.1 0.8 dynamic-slice_bitcast_fusion.2
  66.9 1.5 convert_reduce_fusion.2
  68.3 2.0 fusion.32
  70.4 0.8 dynamic-slice_bitcast_fusion.2
  71.1 1.5 convert_reduce_fusion.2
  72.6 2.0 fusion.32
  74.7 0.8 dynamic-slice_bitcast_fusion.2
  75.4 1.5 convert_reduce_fusion.2
  76.9 2.0 fusion.32
  79.0 0.8 dynamic-slice_bitcast_fusion.2
  79.7 1.5 convert_reduce_fusion.2
  81.2 2.0 fusion.32
  83.2 0.8 dynamic-slice_bitcast_fusion.2
  84.0 1.5 convert_reduce_fusion.2
  85.5 2.0 fusion.32
  87.5 0.1 copy.36
  87.6 0.0 copy-start.1
  87.7 0.4 fusion.16
  88.0 0.8 slice_add_fusion
  88.8 0.0 all-reduce.3.cloned.1.call-update
  88.9 114.5 %all-reduce.3.cloned.1.call-done = f32[16,6272]{1,0:T(8,128)} async-done(((f32[16,6272]{1,0:T(8,128)}), f32[16,6272]{1,0:T(8,128)}) %all-reduce.3.cloned.1.call-update) | async-done | bytes 401424 | tf_op jit(solution)/shard_map/psum | solution.py:106
  203.4 1.9 fusion.7
  (22 shorter events, 0.1 us)
Async XLA Ops:
  6.5 1.4 copy-start
  6.5 196.8 %all-reduce.3.cloned.1.call-start = ((), (), s32[]{:S(2)}) async-start(), calls=%async_computation | async-start | bytes 802816 | tf_op jit(solution)/shard_map/psum | solution.py:106
  9.4 17.1 %collective-permute-start = (f32[16,128]{1,0:T(8,128)S(1)}, f32[16,128]{1,0:T(8,128)S(1)}, u32[]{:S(2)}, u32[]{:S(2)}) collective-permute-start(f32[16,128]{1,0:T(8,128)S(1)} %fusion.10), channel_id=1, source_target_pairs={{0,1},{1,0},{2,3},{3,2},{4,5},{5,4},{6,7},{7,6},{8,9},{9,8},{10,11... | collective-permute-start | bytes 24584 | tf_op jit(solution)/shard_map/ppermute | solution.py:11
  16.0 2.4 %copy-start.4 = (s32[1,2,128]{2,1,0:T(2,128)S(1)}, s32[1,2,128]{2,1,0:T(2,128)}, u32[]{:S(2)}) copy-start(s32[1,2,128]{2,1,0:T(2,128)} %param.12) | copy-start | bytes 3076
  16.1 9.6 %copy-start.3 = (s32[6,6272]{1,0:T(8,128)S(1)}, s32[6,6272]{1,0:T(8,128)}, u32[]{:S(2)}) copy-start(s32[6,6272]{1,0:T(8,128)} %param.13) | copy-start | bytes 451588
  21.9 14.4 %collective-permute-start.5 = (f32[17,128]{0,1:T(8,128)}, f32[17,128]{0,1:T(8,128)}, u32[]{:S(2)}, u32[]{:S(2)}) collective-permute-start(f32[17,128]{0,1:T(8,128)} %get-tuple-element.40), channel_id=1, source_target_pairs={{0,1},{1,2},{2,3},{3,4},{4,5},{5,6},{6,7},{7,8},{8,9},{9,10},{10,1... | collective-permute-start | bytes 26120 | tf_op jit(solution)/shard_map/ppermute | solution.py:22
  24.4 12.8 %collective-permute-start.6 = (f32[17,128]{0,1:T(8,128)}, f32[17,128]{0,1:T(8,128)S(1)}, u32[]{:S(2)}, u32[]{:S(2)}) collective-permute-start(f32[17,128]{0,1:T(8,128)} %get-tuple-element.41), channel_id=1, source_target_pairs={{1,0},{2,1},{3,2},{4,3},{5,4},{6,5},{7,6},{8,7},{9,8},{10,9},{11,1... | collective-permute-start | bytes 26120 | tf_op jit(solution)/shard_map/ppermute | solution.py:23
  26.5 10.8 %collective-permute-start.1 = (f32[16,128]{1,0:T(8,128)S(1)}, f32[16,128]{1,0:T(8,128)}, u32[]{:S(2)}, u32[]{:S(2)}) collective-permute-start(f32[16,128]{1,0:T(8,128)S(1)} %add.68), channel_id=1, source_target_pairs={{0,2},{1,3},{2,0},{3,1},{4,6},{5,7},{6,4},{7,5},{8,10},{9,11},{10,... | collective-permute-start | bytes 24584 | tf_op jit(solution)/shard_map/ppermute | solution.py:11
  38.0 9.0 %collective-permute-start.2 = (f32[16,128]{1,0:T(8,128)S(1)}, f32[16,128]{1,0:T(8,128)S(1)}, u32[]{:S(2)}, u32[]{:S(2)}) collective-permute-start(f32[16,128]{1,0:T(8,128)S(1)} %add.69), channel_id=1, source_target_pairs={{0,4},{1,5},{2,6},{3,7},{4,0},{5,1},{6,2},{7,3},{8,12},{9,13},{10,... | collective-permute-start | bytes 24584 | tf_op jit(solution)/shard_map/ppermute | solution.py:11
  47.0 5.9 %collective-permute-start.3 = (f32[16,128]{1,0:T(8,128)S(1)}, f32[16,128]{1,0:T(8,128)S(1)}, u32[]{:S(2)}, u32[]{:S(2)}) collective-permute-start(f32[16,128]{1,0:T(8,128)S(1)} %add.70), channel_id=1, source_target_pairs={{0,8},{1,9},{2,10},{3,11},{4,12},{5,13},{6,14},{7,15},{8,0},{9,1},... | collective-permute-start | bytes 24584 | tf_op jit(solution)/shard_map/ppermute | solution.py:11
  51.1 6.4 %copy-start.2 = (f32[7,7,17,128]{3,2,1,0:T(8,128)S(1)}, f32[7,7,17,128]{3,2,1,0:T(8,128)}, u32[]{:S(2)}) copy-start(f32[7,7,17,128]{3,2,1,0:T(8,128)} %custom-call.2) | copy-start | bytes 1279492
  52.9 34.8 %collective-permute-start.4 = (f32[16,128]{1,0:T(8,128)S(1)}, f32[16,128]{1,0:T(8,128)S(1)}, u32[]{:S(2)}, u32[]{:S(2)}) collective-permute-start(f32[16,128]{1,0:T(8,128)S(1)} %add.71), channel_id=1, source_target_pairs={{0,16},{1,17},{2,18},{3,19},{4,20},{5,21},{6,22},{7,23},{8,24},{9,... | collective-permute-start | bytes 24584 | tf_op jit(solution)/shard_map/ppermute | solution.py:11
  87.6 115.8 %copy-start.1 = (bf16[16,6272]{1,0:T(8,128)(2,1)S(1)}, bf16[16,6272]{1,0:T(8,128)(2,1)}, u32[]{:S(2)}) copy-start(bf16[16,6272]{1,0:T(8,128)(2,1)} %param.9) | copy-start | bytes 602116
Sparse Core Ops, SparseCore 0:
  89.0 114.3 all-reduce.2
